TPU v7x, 256 devices: a whole 4x4x8 slice. The times are simulated.
256 devices in a mesh: dm: 32 (over x_lo, z, core), beam: 8 (over y, x_hi).
Axes of the slice: x: 4 (x_hi: 2, x_lo: 2; x = x_hi * 2 + x_lo), y: 4, z: 8, core: 2. Of those that a mesh axis runs over, the one named last changes fastest.
Arguments:
- voltages: bfloat16 [4096, 8, 2, 256], P(('beam', 'dm')), may hold values from -6 to 6
- responses: bfloat16 [128, 4096, 2, 256], P('dm', 'beam'), may hold values from -6 to 6
- chirp_len: int32 [128], P('dm'), may hold values from 1 to 128, as said below
Outputs:
- detected: bfloat16 [128, 8, 262144], P('dm', 'beam')
Inputs may be any that keep to these rules, and one draw needn't show every extreme that they name: `chirp_len`: some trial has the longest chirp 256 // 2 and some trial a chirp of 1 sample.
All inputs are finite; a program needn't handle non-finite values.
Results may differ from a plain program's by a relative error of at most 0.0054.
Values may be sent and summed in bfloat16 or wider, within the bound.
No kernel may reach another device: no remote copies, remote signals or barrier semaphores. Data moves between devices by JAX's collectives and lax.ppermute only.
A program may use at most 128 MiB of HBM per device.

v0:
```python
import math
import jax
import jax.numpy as jnp
from jax import lax
from jax.sharding import PartitionSpec as P

RATE = 4


def dft_tables(length):
    sample = jnp.arange(length, dtype=jnp.int32)
    phases = sample[:, None] * sample[None, :] % length
    angles = phases.astype(jnp.float32) * (2.0 * math.pi / length)
    cosine = jnp.cos(angles) / math.sqrt(length)
    sine_part = jnp.sin(angles) / math.sqrt(length)
    forward = jnp.concatenate(
        [jnp.concatenate([cosine, -sine_part], 1), jnp.concatenate([sine_part, cosine], 1)], 0
    )
    backward = jnp.concatenate(
        [jnp.concatenate([cosine, sine_part], 1), jnp.concatenate([-sine_part, cosine], 1)], 0
    )
    return (forward.astype(jnp.bfloat16), backward.astype(jnp.bfloat16))


def spectrum(signal, forward):
    length = signal.shape[-1]
    flattened = signal.reshape(-1, 2 * length)
    result = jnp.dot(flattened, forward, preferred_element_type=jnp.float32)
    return result.astype(jnp.bfloat16).reshape(signal.shape)


def detect(spectra, response, lengths, backward, rate):
    chans = spectra.shape[0]
    beam_count = spectra.shape[1]
    length = spectra.shape[-1]
    samples_out = length // rate
    spec_re = spectra[:, :, 0, :].astype(jnp.float32)
    spec_im = spectra[:, :, 1, :].astype(jnp.float32)
    sample = jnp.arange(length, dtype=jnp.int32)

    def one_trial(trial):
        filter_row, chirp = trial
        resp_re = filter_row[:, 0, :].astype(jnp.float32)[:, None, :]
        resp_im = filter_row[:, 1, :].astype(jnp.float32)[:, None, :]
        real_part = resp_re * spec_re - resp_im * spec_im
        imag_part = resp_re * spec_im + resp_im * spec_re
        joined = jnp.concatenate([real_part, imag_part], -1).astype(jnp.bfloat16)
        series = jnp.dot(
            joined.reshape(-1, 2 * length), backward, preferred_element_type=jnp.float32
        )
        series = series.reshape(chans, beam_count, 2 * length)
        powers = series[..., :length] ** 2 + series[..., length:] ** 2
        valid_mask = sample >= chirp
        powers = jnp.where(valid_mask[None, None, :], powers, jnp.float32(0.0))
        binned = powers.reshape(chans, beam_count, samples_out, rate).sum(-1) / rate
        return jnp.transpose(binned, (1, 0, 2)).astype(jnp.bfloat16)

    return lax.map(one_trial, (response, lengths))


def shards(voltages, responses, chirp_len):
    length = voltages.shape[-1]
    forward, backward = dft_tables(length)
    trial_count = responses.shape[0]
    prepared = spectrum(lax.all_gather(voltages, "dm", axis=0, tiled=True), forward)
    detected = detect(prepared, responses, chirp_len, backward, RATE)
    flattened = detected.reshape(trial_count, detected.shape[1], -1)
    return lax.all_to_all(flattened, "beam", split_axis=1, concat_axis=2, tiled=True)


def solution(mesh):
    placed = (P(("beam", "dm"), None, None, None), P("dm", "beam", None, None), P("dm"))
    return jax.shard_map(
        shards, mesh=mesh, in_specs=placed, out_specs=P("dm", "beam", None), check_vma=False
    )
```

profile of v0, /device:TPU:1, one launch (start us, length us, event | category | flops | bytes accessed | tf_op | source)
XLA Modules:
  0.0 263.4 jit_solution(4098460005403602583)
XLA Ops:
  6.5 0.0 all-gather.2.cloned.1.call-start
  6.5 1.6 copy.11
  8.1 0.0 all-gather.2.cloned.1.call-update
  8.1 1.0 fusion.26
  9.1 1.1 negate_convert_fusion
  10.2 0.8 fusion.17
  11.1 68.8 %all-gather.2.cloned.1.call-done = bf16[512,8,2,256]{3,1,2,0:T(8,128)(2,1)} async-done(((bf16[16,8,2,256]{3,1,2,0:T(8,128)(2,1)}), bf16[512,8,2,256]{3,1,2,0:T(8,128)(2,1)}) %all-gather.2.cloned.1.call-update) | async-done | bytes 4194320 | tf_op jit(solution)/shard_map/all_gather | solution.py:65
  79.9 6.5 %fusion.14 = bf16[4096,512]{0,1:T(8,128)(2,1)} fusion(bf16[4096,512]{1,0:T(8,128)(2,1)} %bitcast.54, bf16[256,256]{0,1:T(8,128)(2,1)S(1)} %get-tuple-element.106, bf16[256,256]{0,1:T(8,128)(2,1)S(1)} %fusion.26, bf16[256,256]{0,1:T(8,128)(2,1)S(1)} %get-tuple-element.105), kind=kOutput, calls=%fused_computation.24 | convolution fusion | flops 2151677952 | bytes 8781824 | tf_op jit(solution)/shard_map/dot_general | solution.py:28
  86.4 6.5 %copy.12 = bf16[4096,512]{1,0:T(8,128)(2,1)} copy(bf16[4096,512]{0,1:T(8,128)(2,1)} %fusion.14) | data formatting | bytes 8388608 | tf_op jit(solution)/shard_map/convert_element_type | solution.py:29
  92.9 7.0 %reshape.32 = bf16[512,8,2,256]{3,2,1,0:T(2,128)(2,1)} reshape(bf16[4096,512]{1,0:T(8,128)(2,1)} %copy.12) | data formatting | bytes 8388608 | tf_op jit(solution)/shard_map/reshape | solution.py:29
  99.9 8.8 %slice_convert_fusion = (f32[512,8,1,256]{3,2,1,0:T(1,128)S(1)}, f32[512,8,1,256]{3,2,1,0:T(1,128)S(1)}) fusion(bf16[512,8,2,256]{3,2,1,0:T(2,128)(2,1)} %reshape.32), kind=kLoop, calls=%fused_computation.25 | loop fusion | flops 2097152 | bytes 12582912 | tf_op jit(solution)/shard_map/convert_element_type | solution.py:38
  108.7 3.3 %copy.27 = f32[512,8,1,256]{3,0,1,2:T(8,128)} copy(f32[512,8,1,256]{3,2,1,0:T(1,128)S(1)} %get-tuple-element.103) | data formatting | bytes 8388608
  111.9 0.0 copy-start
  111.9 3.2 %copy.28 = f32[512,8,1,256]{3,0,1,2:T(8,128)} copy(f32[512,8,1,256]{3,2,1,0:T(1,128)S(1)} %get-tuple-element.104) | data formatting | bytes 8388608
  115.2 0.0 copy-done
  115.2 96.9 %while.11 = (s32[]{:T(128)}, bf16[4,8,512,64]{2,3,1,0:T(8,128)(2,1)S(1)}, s32[4]{0:T(128)S(1)}, bf16[4,512,2,256]{3,2,1,0:T(2,128)(2,1)}, f32[512,8,256]{2,0,1:T...) while((s32[]{:T(128)}, ...), condition=%wide.region_2.3_spmd.clone, body=%wide.region_0.2_spmd.clone.sunk | while | flops 2170028288 | bytes 58196600 | solution.py:58
  115.2 1.4 constant_dynamic-slice_fusion.2
  116.6 0.1 copy.30
  116.7 0.1 fusion.37
  116.7 4.8 %subtract_convert_fusion.2 = (bf16[512,8,256]{2,0,1:T(8,128)(2,1)S(1)}, bf16[512,8,256]{2,0,1:T(8,128)(2,1)S(1)}) fusion(f32[512,8,256]{2,0,1:T(8,128)} %get-tuple-element.181, f32[512,8,256]{2,0,1:T(8,128)} %get-tuple-element.180, f32[512,256]{1,0:T(8,128)S(1)} %get-tuple-element.154, f32[512,256]{1,0:T(8,128)S(1)} %get-tuple-element.155), kind=kLoop, calls=%fused_computation.10.clone.1 | loop fusion | flops 8388608 | bytes 13631488 | tf_op jit(solution)/shard_map/convert.2
  121.5 3.4 %fusion.38 = f32[512,8,512]{0,2,1:T(8,128)S(1)} fusion(bf16[512,8,256]{2,0,1:T(8,128)(2,1)S(1)} %get-tuple-element.156, bf16[512,8,256]{2,0,1:T(8,128)(2,1)S(1)} %get-tuple-element.157, bf16[512,512]{0,1:T(8,128)(2,1)} %get-tuple-element.182), kind=kOutput, calls=%fused_computation.5.clone.1 | convolution fusion | flops 2155872256 | bytes 13107200 | tf_op jit(solution)/shard_map/while/body/eval_jaxpr/dot_general | solution.py:48
  124.9 0.6 dynamic_slice.14
  125.5 0.6 iota_compare_fusion.2
  126.2 3.1 %fusion.39 = f32[512,8,256]{0,2,1:T(8,128)} fusion(f32[512,8,512]{0,2,1:T(8,128)S(1)} %fusion.38, pred[256]{0:T(512)(128)(4,1)S(1)} %iota_compare_fusion.2), kind=kLoop, calls=%fused_computation.3.clone.1 | loop fusion | flops 4194304 | bytes 12583168 | tf_op jit(solution)/shard_map/while/body/eval_jaxpr/jit(_where)/select_n | solution.py:54
  129.3 5.2 %reshape.44 = f32[512,8,64,4]{0,3,2,1:T(4,128)} reshape(f32[512,8,256]{0,2,1:T(8,128)} %fusion.39) | data formatting | bytes 8388608 | tf_op jit(solution)/shard_map/while/body/eval_jaxpr/reshape | solution.py:55
  134.5 4.8 %reduce_sum.11 = f32[512,8,64]{0,2,1:T(8,128)S(1)} reduce(f32[512,8,64,4]{0,3,2,1:T(4,128)} %reshape.44, f32[]{:T(128)} %constant.29.clone.3..sunk), dimensions={3}, to_apply=%region_1.1 | reduce | flops 786432 | bytes 5242884 | tf_op jit(solution)/shard_map/while/body/eval_jaxpr/reduce_sum | solution.py:55
  139.3 0.1 fusion.40
  139.4 1.4 constant_dynamic-slice_fusion.2
  140.8 0.1 copy.30
  140.9 0.1 fusion.37
  141.0 4.8 %subtract_convert_fusion.2 = (bf16[512,8,256]{2,0,1:T(8,128)(2,1)S(1)}, bf16[512,8,256]{2,0,1:T(8,128)(2,1)S(1)}) fusion(f32[512,8,256]{2,0,1:T(8,128)} %get-tuple-element.181, f32[512,8,256]{2,0,1:T(8,128)} %get-tuple-element.180, f32[512,256]{1,0:T(8,128)S(1)} %get-tuple-element.154, f32[512,256]{1,0:T(8,128)S(1)} %get-tuple-element.155), kind=kLoop, calls=%fused_computation.10.clone.1 | loop fusion | flops 8388608 | bytes 13631488 | tf_op jit(solution)/shard_map/convert.2
  145.8 3.4 %fusion.38 = f32[512,8,512]{0,2,1:T(8,128)S(1)} fusion(bf16[512,8,256]{2,0,1:T(8,128)(2,1)S(1)} %get-tuple-element.156, bf16[512,8,256]{2,0,1:T(8,128)(2,1)S(1)} %get-tuple-element.157, bf16[512,512]{0,1:T(8,128)(2,1)} %get-tuple-element.182), kind=kOutput, calls=%fused_computation.5.clone.1 | convolution fusion | flops 2155872256 | bytes 13107200 | tf_op jit(solution)/shard_map/while/body/eval_jaxpr/dot_general | solution.py:48
  149.2 0.6 dynamic_slice.14
  149.8 0.6 iota_compare_fusion.2
  150.4 3.1 %fusion.39 = f32[512,8,256]{0,2,1:T(8,128)} fusion(f32[512,8,512]{0,2,1:T(8,128)S(1)} %fusion.38, pred[256]{0:T(512)(128)(4,1)S(1)} %iota_compare_fusion.2), kind=kLoop, calls=%fused_computation.3.clone.1 | loop fusion | flops 4194304 | bytes 12583168 | tf_op jit(solution)/shard_map/while/body/eval_jaxpr/jit(_where)/select_n | solution.py:54
  153.5 5.2 %reshape.44 = f32[512,8,64,4]{0,3,2,1:T(4,128)} reshape(f32[512,8,256]{0,2,1:T(8,128)} %fusion.39) | data formatting | bytes 8388608 | tf_op jit(solution)/shard_map/while/body/eval_jaxpr/reshape | solution.py:55
  158.7 4.8 %reduce_sum.11 = f32[512,8,64]{0,2,1:T(8,128)S(1)} reduce(f32[512,8,64,4]{0,3,2,1:T(4,128)} %reshape.44, f32[]{:T(128)} %constant.29.clone.3..sunk), dimensions={3}, to_apply=%region_1.1 | reduce | flops 786432 | bytes 5242884 | tf_op jit(solution)/shard_map/while/body/eval_jaxpr/reduce_sum | solution.py:55
  163.5 0.1 fusion.40
  163.7 1.4 constant_dynamic-slice_fusion.2
  165.1 0.1 copy.30
  165.1 0.1 fusion.37
  165.2 4.8 %subtract_convert_fusion.2 = (bf16[512,8,256]{2,0,1:T(8,128)(2,1)S(1)}, bf16[512,8,256]{2,0,1:T(8,128)(2,1)S(1)}) fusion(f32[512,8,256]{2,0,1:T(8,128)} %get-tuple-element.181, f32[512,8,256]{2,0,1:T(8,128)} %get-tuple-element.180, f32[512,256]{1,0:T(8,128)S(1)} %get-tuple-element.154, f32[512,256]{1,0:T(8,128)S(1)} %get-tuple-element.155), kind=kLoop, calls=%fused_computation.10.clone.1 | loop fusion | flops 8388608 | bytes 13631488 | tf_op jit(solution)/shard_map/convert.2
  170.0 3.4 %fusion.38 = f32[512,8,512]{0,2,1:T(8,128)S(1)} fusion(bf16[512,8,256]{2,0,1:T(8,128)(2,1)S(1)} %get-tuple-element.156, bf16[512,8,256]{2,0,1:T(8,128)(2,1)S(1)} %get-tuple-element.157, bf16[512,512]{0,1:T(8,128)(2,1)} %get-tuple-element.182), kind=kOutput, calls=%fused_computation.5.clone.1 | convolution fusion | flops 2155872256 | bytes 13107200 | tf_op jit(solution)/shard_map/while/body/eval_jaxpr/dot_general | solution.py:48
  173.4 0.6 dynamic_slice.14
  174.0 0.6 iota_compare_fusion.2
  174.7 3.1 %fusion.39 = f32[512,8,256]{0,2,1:T(8,128)} fusion(f32[512,8,512]{0,2,1:T(8,128)S(1)} %fusion.38, pred[256]{0:T(512)(128)(4,1)S(1)} %iota_compare_fusion.2), kind=kLoop, calls=%fused_computation.3.clone.1 | loop fusion | flops 4194304 | bytes 12583168 | tf_op jit(solution)/shard_map/while/body/eval_jaxpr/jit(_where)/select_n | solution.py:54
  177.8 5.2 %reshape.44 = f32[512,8,64,4]{0,3,2,1:T(4,128)} reshape(f32[512,8,256]{0,2,1:T(8,128)} %fusion.39) | data formatting | bytes 8388608 | tf_op jit(solution)/shard_map/while/body/eval_jaxpr/reshape | solution.py:55
  183.0 4.8 %reduce_sum.11 = f32[512,8,64]{0,2,1:T(8,128)S(1)} reduce(f32[512,8,64,4]{0,3,2,1:T(4,128)} %reshape.44, f32[]{:T(128)} %constant.29.clone.3..sunk), dimensions={3}, to_apply=%region_1.1 | reduce | flops 786432 | bytes 5242884 | tf_op jit(solution)/shard_map/while/body/eval_jaxpr/reduce_sum | solution.py:55
  187.7 0.1 fusion.40
  187.9 1.4 constant_dynamic-slice_fusion.2
  189.3 0.1 copy.30
  189.4 0.1 fusion.37
  189.5 4.8 %subtract_convert_fusion.2 = (bf16[512,8,256]{2,0,1:T(8,128)(2,1)S(1)}, bf16[512,8,256]{2,0,1:T(8,128)(2,1)S(1)}) fusion(f32[512,8,256]{2,0,1:T(8,128)} %get-tuple-element.181, f32[512,8,256]{2,0,1:T(8,128)} %get-tuple-element.180, f32[512,256]{1,0:T(8,128)S(1)} %get-tuple-element.154, f32[512,256]{1,0:T(8,128)S(1)} %get-tuple-element.155), kind=kLoop, calls=%fused_computation.10.clone.1 | loop fusion | flops 8388608 | bytes 13631488 | tf_op jit(solution)/shard_map/convert.2
  194.2 3.4 %fusion.38 = f32[512,8,512]{0,2,1:T(8,128)S(1)} fusion(bf16[512,8,256]{2,0,1:T(8,128)(2,1)S(1)} %get-tuple-element.156, bf16[512,8,256]{2,0,1:T(8,128)(2,1)S(1)} %get-tuple-element.157, bf16[512,512]{0,1:T(8,128)(2,1)} %get-tuple-element.182), kind=kOutput, calls=%fused_computation.5.clone.1 | convolution fusion | flops 2155872256 | bytes 13107200 | tf_op jit(solution)/shard_map/while/body/eval_jaxpr/dot_general | solution.py:48
  197.7 0.6 dynamic_slice.14
  198.3 0.6 iota_compare_fusion.2
  198.9 3.1 %fusion.39 = f32[512,8,256]{0,2,1:T(8,128)} fusion(f32[512,8,512]{0,2,1:T(8,128)S(1)} %fusion.38, pred[256]{0:T(512)(128)(4,1)S(1)} %iota_compare_fusion.2), kind=kLoop, calls=%fused_computation.3.clone.1 | loop fusion | flops 4194304 | bytes 12583168 | tf_op jit(solution)/shard_map/while/body/eval_jaxpr/jit(_where)/select_n | solution.py:54
  202.0 5.2 %reshape.44 = f32[512,8,64,4]{0,3,2,1:T(4,128)} reshape(f32[512,8,256]{0,2,1:T(8,128)} %fusion.39) | data formatting | bytes 8388608 | tf_op jit(solution)/shard_map/while/body/eval_jaxpr/reshape | solution.py:55
  207.2 4.8 %reduce_sum.11 = f32[512,8,64]{0,2,1:T(8,128)S(1)} reduce(f32[512,8,64,4]{0,3,2,1:T(4,128)} %reshape.44, f32[]{:T(128)} %constant.29.clone.3..sunk), dimensions={3}, to_apply=%region_1.1 | reduce | flops 786432 | bytes 5242884 | tf_op jit(solution)/shard_map/while/body/eval_jaxpr/reduce_sum | solution.py:55
  212.0 0.1 fusion.40
  212.1 3.2 %copy.20 = bf16[4,8,512,64]{3,2,0,1:T(8,128)(2,1)} copy(bf16[4,8,512,64]{2,3,1,0:T(8,128)(2,1)S(1)} %get-tuple-element.47) | data formatting | bytes 4194304 | tf_op jit(solution)/shard_map/reshape | solution.py:67
  215.3 6.3 %reshape.42 = bf16[4,8,32768]{2,0,1:T(4,128)(2,1)S(1)} reshape(bf16[4,8,512,64]{3,2,0,1:T(8,128)(2,1)} %copy.20) | data formatting | bytes 4194304 | tf_op jit(solution)/shard_map/reshape | solution.py:67
  221.6 33.6 %all_to_all.12 = bf16[4,8,32768]{2,0,1:T(4,128)(2,1)S(1)} all-to-all(bf16[4,8,32768]{2,0,1:T(4,128)(2,1)S(1)} %reshape.42), channel_id=1, replica_groups=mesh['dm'=32,'beam'=8] {'beam'}, dimensions={1} | all-to-all | bytes 4194304 | tf_op jit(solution)/shard_map/all_to_all | solution.py:68
  255.2 1.3 copy.41
  (1 shorter events, 0.0 us)
Async XLA Ops:
  6.5 73.4 %all-gather.2.cloned.1.call-start = ((), (), s32[]{:S(2)}) async-start(), calls=%async_computation.1 | async-start | bytes 4325376 | tf_op jit(solution)/shard_map/all_gather | solution.py:65
  111.9 3.2 %copy-start = (s32[4]{0:T(128)S(1)}, s32[4]{0:T(128)}, u32[]{:S(2)}) copy-start(s32[4]{0:T(128)} %param.7) | copy-start | bytes 52
Sparse Core Ops, SparseCore 0:
  9.2 70.6 all-gather.1
where the time goes:
time: 265 us; the launch traced here: 263 us
  waiting for transfers between devices  68.8 us (26%)
  other arithmetic  65.7 us (25%)
  local copies, waits for them, and re-layouts  61.3 us (23%)
  blocking collectives  33.6 us (13%)
  matrix products  20.2 us (8%)
  between operations  13.4 us (5%)
    all_gather x1, waiting for transfers between devices, shards(): lax.all_gather(voltages, 'dm', axis=0, tiled=True)  68.8 us
    all_to_all x1, blocking collectives, shards(): lax.all_to_all(flattened, 'beam', split_axis=1, concat_axis=2, tiled=True)  33.6 us
    another operation x6, other arithmetic  21.1 us
    reshape x4, local copies, waits for them, and re-layouts, one_trial(): binned = powers.reshape(chans, beam_count, samples_out, rate).sum(-1) / rate  20.7 us
    reduce_sum x4, other arithmetic, one_trial(): binned = powers.reshape(chans, beam_count, samples_out, rate).sum(-1) / rate  19.1 us
    dot_general x4, matrix products, one_trial(): jnp.dot(joined.reshape(-1, 2 * length), backward, preferred_element_type=...  13.7 us
    select_n x4, other arithmetic, one_trial(): powers = jnp.where(valid_mask[None, None, :], powers, jnp.float32(0.0))  12.5 us
    reshape x2, local copies, waits for them, and re-layouts, shards(): flattened = detected.reshape(trial_count, detected.shape[1], -1)  9.45 us
  transfers between devices with their start and end apart: 1, of which 1 were waited for; matrix products, arithmetic and copies ran while one was open for 1% of the time, Pallas kernels for 0%

commit v1 on v0

--- a/solution.py
+++ b/solution.py
@@ -5,6 +5,13 @@
 from jax.sharding import PartitionSpec as P
 
 RATE = 4
+
+
+def all_by_exchange(value, axis, dim):
+    size = lax.axis_size(axis)
+    parts = jnp.stack([value for _ in range(size)])
+    parts = lax.all_to_all(parts, axis, split_axis=0, concat_axis=0)
+    return jnp.concatenate(parts, axis=dim)
 
 
 def dft_tables(length):
@@ -62,7 +69,7 @@
     length = voltages.shape[-1]
     forward, backward = dft_tables(length)
     trial_count = responses.shape[0]
-    prepared = spectrum(lax.all_gather(voltages, "dm", axis=0, tiled=True), forward)
+    prepared = spectrum(all_by_exchange(voltages, "dm", 0), forward)
     detected = detect(prepared, responses, chirp_len, backward, RATE)
     flattened = detected.reshape(trial_count, detected.shape[1], -1)
     return lax.all_to_all(flattened, "beam", split_axis=1, concat_axis=2, tiled=True)

time: 265 us -> 291 us (1.098)
  waiting for transfers between devices: 68.8 us -> 91.7 us
  between operations: 13.4 us -> 0.06 us
  starting transfers between devices: 0.01 us -> 11.1 us
  local copies, waits for them, and re-layouts: 61.3 us -> 69.4 us
    all_to_all x0 -> x1, waiting for transfers between devices: none -> 91.7 us  [all_by_exchange(): parts = lax.all_to_all(parts, axis, split_axis=0, concat_axis=0)]
    all_gather x1 -> x0, waiting for transfers between devices: 68.8 us -> none  [shards(): lax.all_gather(voltages, 'dm', axis=0, tiled=True)]
    all_to_all x0 -> x1, starting transfers between devices: none -> 11.1 us  [all_by_exchange(): parts = lax.all_to_all(parts, axis, split_axis=0, concat_axis=0)]
    another operation x0 -> x1, local copies, waits for them, and re-layouts: none -> 6.66 us  [all_by_exchange(): parts = jnp.stack([value for _ in range(size)])]
where the time goes in v1:
time: 291 us; the launch traced here: 290 us
  waiting for transfers between devices  91.7 us (32%)
  local copies, waits for them, and re-layouts  69.4 us (24%)
  other arithmetic  65.6 us (23%)
  blocking collectives  33.6 us (12%)
  matrix products  18 us (6%)
  starting transfers between devices  11.1 us (4%)
    all_to_all x1, waiting for transfers between devices, all_by_exchange(): parts = lax.all_to_all(parts, axis, split_axis=0, concat_axis=0)  91.7 us
    all_to_all x1, blocking collectives, shards(): lax.all_to_all(flattened, 'beam', split_axis=1, concat_axis=2, tiled=True)  33.6 us
    another operation x6, other arithmetic  21.1 us
    reshape x4, local copies, waits for them, and re-layouts, one_trial(): binned = powers.reshape(chans, beam_count, samples_out, rate).sum(-1) / rate  20.7 us
    reduce_sum x4, other arithmetic, one_trial(): binned = powers.reshape(chans, beam_count, samples_out, rate).sum(-1) / rate  19.1 us
    dot_general x4, matrix products, one_trial(): jnp.dot(joined.reshape(-1, 2 * length), backward, preferred_element_type=...  13.7 us
    select_n x4, other arithmetic, one_trial(): powers = jnp.where(valid_mask[None, None, :], powers, jnp.float32(0.0))  12.4 us
    all_to_all x1, starting transfers between devices, all_by_exchange(): parts = lax.all_to_all(parts, axis, split_axis=0, concat_axis=0)  11.1 us
  transfers between devices with their start and end apart: 1, of which 1 were waited for; matrix products, arithmetic and copies ran while one was open for 1% of the time, Pallas kernels for 0%

profile of v1, /device:TPU:1, one launch (start us, length us, event | category | flops | bytes accessed | tf_op | source)
XLA Modules:
  0.0 289.8 jit_solution(7090966554814448251)
XLA Ops:
  0.0 6.7 %stack.2 = bf16[32,16,8,2,256]{4,3,2,1,0:T(2,128)(2,1)} broadcast(bf16[16,8,2,256]{3,2,1,0:T(2,128)(2,1)} %param.5), dimensions={1,2,3,4} | broadcast | bytes 4325376 | tf_op jit(solution)/shard_map/stack | solution.py:12
  6.7 11.1 %all-to-all-start = ((bf16[32,16,8,2,256]{4,3,2,1,0:T(2,128)(2,1)}), bf16[32,16,8,2,256]{4,3,2,1,0:T(2,128)(2,1)}, u32[]{:S(2)}, u32[]{:S(2)}) async-start(bf16[32,16,8,2,256]{4,3,2,1,0:T(2,128)(2,1)} %stack.2), calls=%async_computation | async-start | bytes 8388608 | tf_op jit(solution)/shard_map/all_to_all | solution.py:13
  17.8 1.0 fusion.26
  18.8 1.1 negate_convert_fusion
  19.9 0.8 fusion.17
  20.7 91.7 %all-to-all-done = bf16[32,16,8,2,256]{4,3,2,1,0:T(2,128)(2,1)} async-done(((bf16[32,16,8,2,256]{4,3,2,1,0:T(2,128)(2,1)}), bf16[32,16,8,2,256]{4,3,2,1,0:T(2,128)(2,1)}, u32[]{:S(2)}, u32[]{:S(2)}) %all-to-all-start) | async-done | bytes 4194336 | tf_op jit(solution)/shard_map/all_to_all | solution.py:13
  112.5 2.9 %copy.22 = bf16[512,8,2,256]{3,1,2,0:T(8,128)(2,1)S(1)} copy(bf16[512,8,2,256]{3,2,1,0:T(2,128)(2,1)} %bitcast.16) | data formatting | bytes 8388608
  115.4 4.4 %fusion.14 = bf16[4096,512]{0,1:T(8,128)(2,1)} fusion(bf16[4096,512]{1,0:T(8,128)(2,1)S(1)} %bitcast.56, bf16[256,256]{0,1:T(8,128)(2,1)S(1)} %get-tuple-element.106, bf16[256,256]{0,1:T(8,128)(2,1)S(1)} %fusion.26, bf16[256,256]{0,1:T(8,128)(2,1)S(1)} %get-tuple-element.105), kind=kOutput, calls=%fused_computation.24 | convolution fusion | flops 2151677952 | bytes 8781824 | tf_op jit(solution)/shard_map/dot_general | solution.py:35
  119.7 6.5 %copy.11 = bf16[4096,512]{1,0:T(8,128)(2,1)} copy(bf16[4096,512]{0,1:T(8,128)(2,1)} %fusion.14) | data formatting | bytes 8388608 | tf_op jit(solution)/shard_map/convert_element_type | solution.py:36
  126.2 7.0 %reshape.30 = bf16[512,8,2,256]{3,2,1,0:T(2,128)(2,1)} reshape(bf16[4096,512]{1,0:T(8,128)(2,1)} %copy.11) | data formatting | bytes 8388608 | tf_op jit(solution)/shard_map/reshape | solution.py:36
  133.2 8.8 %slice_convert_fusion = (f32[512,8,1,256]{3,2,1,0:T(1,128)S(1)}, f32[512,8,1,256]{3,2,1,0:T(1,128)S(1)}) fusion(bf16[512,8,2,256]{3,2,1,0:T(2,128)(2,1)} %reshape.30), kind=kLoop, calls=%fused_computation.25 | loop fusion | flops 2097152 | bytes 12582912 | tf_op jit(solution)/shard_map/convert_element_type | solution.py:45
  142.0 3.3 %copy.27 = f32[512,8,1,256]{3,0,1,2:T(8,128)} copy(f32[512,8,1,256]{3,2,1,0:T(1,128)S(1)} %get-tuple-element.103) | data formatting | bytes 8388608
  145.2 0.0 copy-start
  145.2 3.2 %copy.28 = f32[512,8,1,256]{3,0,1,2:T(8,128)} copy(f32[512,8,1,256]{3,2,1,0:T(1,128)S(1)} %get-tuple-element.104) | data formatting | bytes 8388608
  148.5 0.0 copy-done
  148.5 97.0 %while.11 = (s32[]{:T(128)}, bf16[4,8,512,64]{2,3,1,0:T(8,128)(2,1)S(1)}, s32[4]{0:T(128)S(1)}, bf16[4,512,2,256]{3,2,1,0:T(2,128)(2,1)}, f32[512,8,256]{2,0,1:T...) while((s32[]{:T(128)}, ...), condition=%wide.region_2.3_spmd.clone, body=%wide.region_0.2_spmd.clone.sunk | while | flops 2170028288 | bytes 58196600 | solution.py:65
  148.5 1.4 constant_dynamic-slice_fusion.2
  149.9 0.1 copy.30
  149.9 0.1 fusion.37
  150.0 4.8 %subtract_convert_fusion.2 = (bf16[512,8,256]{2,0,1:T(8,128)(2,1)S(1)}, bf16[512,8,256]{2,0,1:T(8,128)(2,1)S(1)}) fusion(f32[512,8,256]{2,0,1:T(8,128)} %get-tuple-element.181, f32[512,8,256]{2,0,1:T(8,128)} %get-tuple-element.180, f32[512,256]{1,0:T(8,128)S(1)} %get-tuple-element.154, f32[512,256]{1,0:T(8,128)S(1)} %get-tuple-element.155), kind=kLoop, calls=%fused_computation.10.clone.1 | loop fusion | flops 8388608 | bytes 13631488 | tf_op jit(solution)/shard_map/convert.2
  154.8 3.4 %fusion.38 = f32[512,8,512]{0,2,1:T(8,128)S(1)} fusion(bf16[512,8,256]{2,0,1:T(8,128)(2,1)S(1)} %get-tuple-element.156, bf16[512,8,256]{2,0,1:T(8,128)(2,1)S(1)} %get-tuple-element.157, bf16[512,512]{0,1:T(8,128)(2,1)} %get-tuple-element.182), kind=kOutput, calls=%fused_computation.5.clone.1 | convolution fusion | flops 2155872256 | bytes 13107200 | tf_op jit(solution)/shard_map/while/body/eval_jaxpr/dot_general | solution.py:55
  158.2 0.6 dynamic_slice.14
  158.9 0.6 iota_compare_fusion.2
  159.5 3.1 %fusion.39 = f32[512,8,256]{0,2,1:T(8,128)} fusion(f32[512,8,512]{0,2,1:T(8,128)S(1)} %fusion.38, pred[256]{0:T(512)(128)(4,1)S(1)} %iota_compare_fusion.2), kind=kLoop, calls=%fused_computation.3.clone.1 | loop fusion | flops 4194304 | bytes 12583168 | tf_op jit(solution)/shard_map/while/body/eval_jaxpr/jit(_where)/select_n | solution.py:61
  162.6 5.2 %reshape.42 = f32[512,8,64,4]{0,3,2,1:T(4,128)} reshape(f32[512,8,256]{0,2,1:T(8,128)} %fusion.39) | data formatting | bytes 8388608 | tf_op jit(solution)/shard_map/while/body/eval_jaxpr/reshape | solution.py:62
  167.8 4.8 %reduce_sum.11 = f32[512,8,64]{0,2,1:T(8,128)S(1)} reduce(f32[512,8,64,4]{0,3,2,1:T(4,128)} %reshape.42, f32[]{:T(128)} %constant.29.clone.3..sunk), dimensions={3}, to_apply=%region_1.1 | reduce | flops 786432 | bytes 5242884 | tf_op jit(solution)/shard_map/while/body/eval_jaxpr/reduce_sum | solution.py:62
  172.6 0.1 fusion.40
  172.7 1.4 constant_dynamic-slice_fusion.2
  174.1 0.1 copy.30
  174.2 0.1 fusion.37
  174.3 4.8 %subtract_convert_fusion.2 = (bf16[512,8,256]{2,0,1:T(8,128)(2,1)S(1)}, bf16[512,8,256]{2,0,1:T(8,128)(2,1)S(1)}) fusion(f32[512,8,256]{2,0,1:T(8,128)} %get-tuple-element.181, f32[512,8,256]{2,0,1:T(8,128)} %get-tuple-element.180, f32[512,256]{1,0:T(8,128)S(1)} %get-tuple-element.154, f32[512,256]{1,0:T(8,128)S(1)} %get-tuple-element.155), kind=kLoop, calls=%fused_computation.10.clone.1 | loop fusion | flops 8388608 | bytes 13631488 | tf_op jit(solution)/shard_map/convert.2
  179.0 3.4 %fusion.38 = f32[512,8,512]{0,2,1:T(8,128)S(1)} fusion(bf16[512,8,256]{2,0,1:T(8,128)(2,1)S(1)} %get-tuple-element.156, bf16[512,8,256]{2,0,1:T(8,128)(2,1)S(1)} %get-tuple-element.157, bf16[512,512]{0,1:T(8,128)(2,1)} %get-tuple-element.182), kind=kOutput, calls=%fused_computation.5.clone.1 | convolution fusion | flops 2155872256 | bytes 13107200 | tf_op jit(solution)/shard_map/while/body/eval_jaxpr/dot_general | solution.py:55
  182.5 0.6 dynamic_slice.14
  183.1 0.6 iota_compare_fusion.2
  183.7 3.1 %fusion.39 = f32[512,8,256]{0,2,1:T(8,128)} fusion(f32[512,8,512]{0,2,1:T(8,128)S(1)} %fusion.38, pred[256]{0:T(512)(128)(4,1)S(1)} %iota_compare_fusion.2), kind=kLoop, calls=%fused_computation.3.clone.1 | loop fusion | flops 4194304 | bytes 12583168 | tf_op jit(solution)/shard_map/while/body/eval_jaxpr/jit(_where)/select_n | solution.py:61
  186.9 5.2 %reshape.42 = f32[512,8,64,4]{0,3,2,1:T(4,128)} reshape(f32[512,8,256]{0,2,1:T(8,128)} %fusion.39) | data formatting | bytes 8388608 | tf_op jit(solution)/shard_map/while/body/eval_jaxpr/reshape | solution.py:62
  192.0 4.8 %reduce_sum.11 = f32[512,8,64]{0,2,1:T(8,128)S(1)} reduce(f32[512,8,64,4]{0,3,2,1:T(4,128)} %reshape.42, f32[]{:T(128)} %constant.29.clone.3..sunk), dimensions={3}, to_apply=%region_1.1 | reduce | flops 786432 | bytes 5242884 | tf_op jit(solution)/shard_map/while/body/eval_jaxpr/reduce_sum | solution.py:62
  196.8 0.1 fusion.40
  197.0 1.4 constant_dynamic-slice_fusion.2
  198.4 0.1 copy.30
  198.5 0.1 fusion.37
  198.5 4.8 %subtract_convert_fusion.2 = (bf16[512,8,256]{2,0,1:T(8,128)(2,1)S(1)}, bf16[512,8,256]{2,0,1:T(8,128)(2,1)S(1)}) fusion(f32[512,8,256]{2,0,1:T(8,128)} %get-tuple-element.181, f32[512,8,256]{2,0,1:T(8,128)} %get-tuple-element.180, f32[512,256]{1,0:T(8,128)S(1)} %get-tuple-element.154, f32[512,256]{1,0:T(8,128)S(1)} %get-tuple-element.155), kind=kLoop, calls=%fused_computation.10.clone.1 | loop fusion | flops 8388608 | bytes 13631488 | tf_op jit(solution)/shard_map/convert.2
  203.3 3.4 %fusion.38 = f32[512,8,512]{0,2,1:T(8,128)S(1)} fusion(bf16[512,8,256]{2,0,1:T(8,128)(2,1)S(1)} %get-tuple-element.156, bf16[512,8,256]{2,0,1:T(8,128)(2,1)S(1)} %get-tuple-element.157, bf16[512,512]{0,1:T(8,128)(2,1)} %get-tuple-element.182), kind=kOutput, calls=%fused_computation.5.clone.1 | convolution fusion | flops 2155872256 | bytes 13107200 | tf_op jit(solution)/shard_map/while/body/eval_jaxpr/dot_general | solution.py:55
  206.7 0.6 dynamic_slice.14
  207.4 0.6 iota_compare_fusion.2
  208.0 3.1 %fusion.39 = f32[512,8,256]{0,2,1:T(8,128)} fusion(f32[512,8,512]{0,2,1:T(8,128)S(1)} %fusion.38, pred[256]{0:T(512)(128)(4,1)S(1)} %iota_compare_fusion.2), kind=kLoop, calls=%fused_computation.3.clone.1 | loop fusion | flops 4194304 | bytes 12583168 | tf_op jit(solution)/shard_map/while/body/eval_jaxpr/jit(_where)/select_n | solution.py:61
  211.1 5.2 %reshape.42 = f32[512,8,64,4]{0,3,2,1:T(4,128)} reshape(f32[512,8,256]{0,2,1:T(8,128)} %fusion.39) | data formatting | bytes 8388608 | tf_op jit(solution)/shard_map/while/body/eval_jaxpr/reshape | solution.py:62
  216.3 4.8 %reduce_sum.11 = f32[512,8,64]{0,2,1:T(8,128)S(1)} reduce(f32[512,8,64,4]{0,3,2,1:T(4,128)} %reshape.42, f32[]{:T(128)} %constant.29.clone.3..sunk), dimensions={3}, to_apply=%region_1.1 | reduce | flops 786432 | bytes 5242884 | tf_op jit(solution)/shard_map/while/body/eval_jaxpr/reduce_sum | solution.py:62
  221.1 0.1 fusion.40
  221.2 1.4 constant_dynamic-slice_fusion.2
  222.6 0.1 copy.30
  222.7 0.1 fusion.37
  222.8 4.8 %subtract_convert_fusion.2 = (bf16[512,8,256]{2,0,1:T(8,128)(2,1)S(1)}, bf16[512,8,256]{2,0,1:T(8,128)(2,1)S(1)}) fusion(f32[512,8,256]{2,0,1:T(8,128)} %get-tuple-element.181, f32[512,8,256]{2,0,1:T(8,128)} %get-tuple-element.180, f32[512,256]{1,0:T(8,128)S(1)} %get-tuple-element.154, f32[512,256]{1,0:T(8,128)S(1)} %get-tuple-element.155), kind=kLoop, calls=%fused_computation.10.clone.1 | loop fusion | flops 8388608 | bytes 13631488 | tf_op jit(solution)/shard_map/convert.2
  227.6 3.4 %fusion.38 = f32[512,8,512]{0,2,1:T(8,128)S(1)} fusion(bf16[512,8,256]{2,0,1:T(8,128)(2,1)S(1)} %get-tuple-element.156, bf16[512,8,256]{2,0,1:T(8,128)(2,1)S(1)} %get-tuple-element.157, bf16[512,512]{0,1:T(8,128)(2,1)} %get-tuple-element.182), kind=kOutput, calls=%fused_computation.5.clone.1 | convolution fusion | flops 2155872256 | bytes 13107200 | tf_op jit(solution)/shard_map/while/body/eval_jaxpr/dot_general | solution.py:55
  231.0 0.6 dynamic_slice.14
  231.6 0.6 iota_compare_fusion.2
  232.3 3.1 %fusion.39 = f32[512,8,256]{0,2,1:T(8,128)} fusion(f32[512,8,512]{0,2,1:T(8,128)S(1)} %fusion.38, pred[256]{0:T(512)(128)(4,1)S(1)} %iota_compare_fusion.2), kind=kLoop, calls=%fused_computation.3.clone.1 | loop fusion | flops 4194304 | bytes 12583168 | tf_op jit(solution)/shard_map/while/body/eval_jaxpr/jit(_where)/select_n | solution.py:61
  235.4 5.2 %reshape.42 = f32[512,8,64,4]{0,3,2,1:T(4,128)} reshape(f32[512,8,256]{0,2,1:T(8,128)} %fusion.39) | data formatting | bytes 8388608 | tf_op jit(solution)/shard_map/while/body/eval_jaxpr/reshape | solution.py:62
  240.5 4.8 %reduce_sum.11 = f32[512,8,64]{0,2,1:T(8,128)S(1)} reduce(f32[512,8,64,4]{0,3,2,1:T(4,128)} %reshape.42, f32[]{:T(128)} %constant.29.clone.3..sunk), dimensions={3}, to_apply=%region_1.1 | reduce | flops 786432 | bytes 5242884 | tf_op jit(solution)/shard_map/while/body/eval_jaxpr/reduce_sum | solution.py:62
  245.3 0.1 fusion.40
  245.5 3.2 %copy.19 = bf16[4,8,512,64]{3,2,0,1:T(8,128)(2,1)} copy(bf16[4,8,512,64]{2,3,1,0:T(8,128)(2,1)S(1)} %get-tuple-element.47) | data formatting | bytes 4194304 | tf_op jit(solution)/shard_map/reshape | solution.py:74
  248.6 6.3 %reshape.40 = bf16[4,8,32768]{2,0,1:T(4,128)(2,1)S(1)} reshape(bf16[4,8,512,64]{3,2,0,1:T(8,128)(2,1)} %copy.19) | data formatting | bytes 4194304 | tf_op jit(solution)/shard_map/reshape | solution.py:74
  254.9 33.6 %all_to_all.17 = bf16[4,8,32768]{2,0,1:T(4,128)(2,1)S(1)} all-to-all(bf16[4,8,32768]{2,0,1:T(4,128)(2,1)S(1)} %reshape.40), channel_id=1, replica_groups=mesh['dm'=32,'beam'=8] {'beam'}, dimensions={1} | all-to-all | bytes 4194304 | tf_op jit(solution)/shard_map/all_to_all | solution.py:75
  288.5 1.3 copy.41
  (1 shorter events, 0.0 us)
Async XLA Ops:
  6.7 105.8 %all-to-all-start = ((bf16[32,16,8,2,256]{4,3,2,1,0:T(2,128)(2,1)}), bf16[32,16,8,2,256]{4,3,2,1,0:T(2,128)(2,1)}, u32[]{:S(2)}, u32[]{:S(2)}) async-start(bf16[32,16,8,2,256]{4,3,2,1,0:T(2,128)(2,1)} %stack.2), calls=%async_computation | async-start | bytes 8388608 | tf_op jit(solution)/shard_map/all_to_all | solution.py:13
  145.2 3.2 %copy-start = (s32[4]{0:T(128)S(1)}, s32[4]{0:T(128)}, u32[]{:S(2)}) copy-start(s32[4]{0:T(128)} %param.7) | copy-start | bytes 52
